TPU v7x, 256 devices: a whole 4x4x8 slice. The times are simulated.
256 devices in a mesh: batch: 16 (over x_hi, z), dom: 16 (over x_lo, y, core).
Axes of the slice: x: 4 (x_hi: 2, x_lo: 2; x = x_hi * 2 + x_lo), y: 4, z: 8, core: 2. Of those that a mesh axis runs over, the one named last changes fastest.
Arguments:
- inputs: bfloat16 [32, 64, 68, 256], P('batch', 'dom'), may hold values from -70 to 70
- saved_q: bfloat16 [32, 64, 68, 256], P('batch', 'dom'), may hold values from -6.5 to 6.5
- saved_k: bfloat16 [32, 64, 68, 256], P('batch', 'dom'), may hold values from -6.5 to 6.5
- saved_v: bfloat16 [32, 64, 68, 256], P('batch', 'dom'), may hold values from -6 to 6
- attended: bfloat16 [32, 64, 68, 256], P('batch', 'dom'), may hold values from -6 to 6
- out_cot: bfloat16 [32, 64, 68, 256], P('batch', 'dom'), may hold values from -6 to 6
- conv_weight: bfloat16 [9, 256, 256], replicated, may hold values from -0.125 to 0.125
- qkv_weight: bfloat16 [256, 768], replicated, may hold values from -0.375 to 0.375
- out_weight: bfloat16 [256, 256], replicated, may hold values from -0.375 to 0.375
- norm_gain: float32 [256], replicated, may hold values from 0.5 to 1.5
- norm_shift: float32 [256], replicated, may hold values from -2.5 to 2.5
Outputs:
- input_grad: bfloat16 [32, 64, 68, 256], P('batch', 'dom')
- conv_grad: float32 [9, 256, 256], replicated
- qkv_grad: float32 [256, 768], replicated
- out_grad: float32 [256, 256], replicated
- gain_grad: float32 [256], replicated
- shift_grad: float32 [256], replicated
All inputs are finite; a program needn't handle non-finite values.
Results may differ from a plain program's by a relative error of at most 0.011.
Values may be sent and summed in bfloat16 or wider, within the bound.
No kernel may reach another device: no remote copies, remote signals or barrier semaphores. Data moves between devices by JAX's collectives and lax.ppermute only.
A program may use at most 128 MiB of HBM per device.

v0:
```python
import jax
import jax.numpy as jnp
from jax import lax
from jax.sharding import PartitionSpec as P

HEADS = 1
GROUPS = 32
EPSILON = 1e-05


def with_halo(cells, sides, width):
    for axis, dim in sides:
        count = lax.axis_size(axis)
        ends = count - 1
        head = lax.slice_in_dim(cells, 0, width, axis=dim)
        tail = lax.slice_in_dim(cells, cells.shape[dim] - width, cells.shape[dim], axis=dim)
        cells = jnp.concatenate(
            [
                lax.ppermute(tail, axis, [(i, (i + 1) % count) for i in range(ends)]),
                cells,
                lax.ppermute(head, axis, [((i + 1) % count, i) for i in range(ends)]),
            ],
            axis=dim,
        )
    return cells


def dom_psum(values):
    count = lax.axis_size("dom")
    step = 1
    while step < count:
        values = values + lax.ppermute(values, "dom", [(i, i ^ step) for i in range(count)])
        step *= 2
    return values


def dom_gather(values):
    count = lax.axis_size("dom")
    me = lax.axis_index("dom")
    values = values[None]
    step = 1
    while step < count:
        got = lax.ppermute(values, "dom", [(i, i ^ step) for i in range(count)])
        upper = me // step % 2 == 1
        values = jnp.where(upper, jnp.concatenate([got, values]), jnp.concatenate([values, got]))
        step *= 2
    return values


MESH_AXES = ("batch", "dom")
CORE0_BITS = (1, 3, 4, 2, 7, 5, 6)
CORE1_BITS = (4, 1, 3, 5, 2, 7, 6)


def mesh_psum(values):
    sizes = (lax.axis_size("batch"), lax.axis_size("dom"))
    if sizes != (16, 16):
        return lax.psum(values, MESH_AXES)
    count = 256
    me = lax.axis_index(MESH_AXES)
    core = me % 2
    steps = [(0, 0)] + list(zip(CORE0_BITS, CORE1_BITS))
    chosen = []
    for bit0, bit1 in steps:
        half = values.shape[0] // 2
        upper = jnp.where(core == 0, me >> bit0 & 1, me >> bit1 & 1) == 1
        low, high = (values[:half], values[half:])
        send = jnp.where(upper, low, high)
        keep = jnp.where(upper, high, low)
        pairs = [(i, i ^ 1 << (bit0 if i % 2 == 0 else bit1)) for i in range(count)]
        values = keep + lax.ppermute(send, MESH_AXES, pairs)
        chosen.append((upper, pairs))
    for upper, pairs in reversed(chosen):
        got = lax.ppermute(values, MESH_AXES, pairs)
        values = jnp.where(upper, jnp.concatenate([got, values]), jnp.concatenate([values, got]))
    return values


def per_channel(values, group_width):
    return jnp.repeat(values, group_width, axis=-1)[:, None, None, :]


def body(
    inputs,
    saved_q,
    saved_k,
    saved_v,
    attended,
    out_cot,
    conv_weight,
    qkv_weight,
    out_weight,
    norm_gain,
    norm_shift,
):
    samples, row_count, col_count, chan_count = inputs.shape
    tok_count = row_count * col_count
    group_width = chan_count // GROUPS
    head_width = chan_count // HEADS
    score_scale = head_width ** (-0.5)
    count = row_count * col_count * group_width * lax.axis_size("dom")
    f32 = jnp.float32
    bf16 = jnp.bfloat16
    input_wide = inputs.astype(f32)
    grouped = input_wide.reshape(samples, row_count, col_count, GROUPS, group_width)
    group_sums = dom_psum(jnp.stack([grouped.sum((1, 2, 4)), (grouped * grouped).sum((1, 2, 4))]))
    group_mean = group_sums[0] / count
    group_var = group_sums[1] / count - group_mean * group_mean
    inv_std = lax.rsqrt(group_var + EPSILON)
    normed = (input_wide - per_channel(group_mean, group_width)) * per_channel(inv_std, group_width)
    pre_act = normed * norm_gain + norm_shift
    sigmoid_pre = jax.nn.sigmoid(pre_act)
    activated = (pre_act * sigmoid_pre).astype(bf16)
    padded = with_halo(activated, (("dom", 1),), 1)
    padded = jnp.pad(padded, ((0, 0), (0, 0), (1, 1), (0, 0)))

    def shifted(source, row_start, col_start):
        return source[
            :, row_start : row_start + row_count, col_start : col_start + col_count, :
        ].reshape(-1, chan_count)

    conv_sum = input_wide.reshape(-1, chan_count)
    for tap_index in range(9):
        row_off = tap_index // 3 - 1
        col_off = tap_index % 3 - 1
        conv_sum = conv_sum + jnp.dot(
            shifted(padded, 1 + row_off, 1 + col_off),
            conv_weight[tap_index],
            preferred_element_type=f32,
        )
    residual = conv_sum.astype(bf16)
    out_flat = out_cot.reshape(-1, chan_count)
    attended_flat = attended.reshape(-1, chan_count)
    out_grad = jnp.einsum("nc,nd->cd", attended_flat, out_flat, preferred_element_type=f32)
    d_attended = jnp.einsum("nd,cd->nc", out_flat, out_weight, preferred_element_type=f32).astype(
        bf16
    )

    def split_heads(values):
        return values.reshape(samples, -1, HEADS, head_width)

    def scores(left, right):
        return jnp.einsum("sqhd,skhd->shqk", left, right, preferred_element_type=f32) * score_scale

    q_rows = saved_q.reshape(samples, tok_count, chan_count)
    k_rows = saved_k.reshape(samples, tok_count, chan_count)
    v_rows = saved_v.reshape(samples, tok_count, chan_count)
    do_rows = d_attended.reshape(samples, tok_count, chan_count)
    q_heads = split_heads(q_rows)
    k_heads = split_heads(k_rows)
    v_heads = split_heads(v_rows)
    do_heads = split_heads(do_rows)
    row_dot = jnp.einsum(
        "sqhd,sqhd->sqh",
        split_heads(attended.reshape(samples, tok_count, chan_count)),
        do_heads,
        preferred_element_type=f32,
    )
    row_dot_t = row_dot.transpose(0, 2, 1)

    def grad_terms(query_heads, dout_heads, key_heads, value_heads, log_norm_t, dot_t):
        softmax_p = jnp.exp(scores(query_heads, key_heads) - log_norm_t[..., None])
        d_probs = jnp.einsum("sqhd,skhd->shqk", dout_heads, value_heads, preferred_element_type=f32)
        d_scores = (softmax_p * (d_probs - dot_t[..., None])).astype(bf16)
        return (softmax_p.astype(bf16), d_scores)

    row_max = jnp.full((samples, HEADS, tok_count), -jnp.inf, f32)
    row_total = jnp.zeros((samples, HEADS, tok_count), f32)
    logits = scores(q_heads, split_heads(lax.all_gather(k_rows, "dom", axis=1, tiled=True)))
    new_max = logits.max(-1)
    row_total = row_total * jnp.exp(row_max - new_max) + jnp.exp(logits - new_max[..., None]).sum(
        -1
    )
    row_max, row_total = (new_max, row_total)
    log_norm = row_max + jnp.log(row_total)
    shard_piece = (
        lax.all_gather(k_rows, "dom", axis=1, tiled=True),
        lax.all_gather(v_rows, "dom", axis=1, tiled=True),
    )
    key_heads = split_heads(shard_piece[0])
    value_heads = split_heads(shard_piece[1])
    p_half, d_scores = grad_terms(q_heads, do_heads, key_heads, value_heads, log_norm, row_dot_t)
    q_accum = jnp.einsum("shqk,skhd->sqhd", d_scores, key_heads, preferred_element_type=f32)
    stats_local = dom_gather(jnp.stack([log_norm.transpose(0, 2, 1), row_dot]))
    stats_all = stats_local.transpose(1, 2, 0, 3, 4).reshape(2, samples, -1, HEADS)
    shard_piece = (
        lax.all_gather(q_rows, "dom", axis=1, tiled=True),
        lax.all_gather(do_rows, "dom", axis=1, tiled=True),
    )
    query_heads = split_heads(shard_piece[0])
    dout_heads = split_heads(shard_piece[1])
    norm_piece = stats_all[0].transpose(0, 2, 1)
    dot_piece = stats_all[1].transpose(0, 2, 1)
    p_half, d_scores = grad_terms(query_heads, dout_heads, k_heads, v_heads, norm_piece, dot_piece)
    k_accum = jnp.einsum("shqk,sqhd->skhd", d_scores, query_heads, preferred_element_type=f32)
    v_accum = jnp.einsum("shqk,sqhd->skhd", p_half, dout_heads, preferred_element_type=f32)
    k_accum, v_accum = (k_accum, v_accum)
    k_grad = (k_accum * score_scale).astype(bf16).reshape(samples, tok_count, chan_count)
    v_grad = v_accum.astype(bf16).reshape(samples, tok_count, chan_count)
    q_grad = (q_accum * score_scale).astype(bf16).reshape(samples, tok_count, chan_count)
    proj_grad = jnp.concatenate([q_grad, k_grad, v_grad], axis=-1).reshape(-1, 3 * chan_count)
    qkv_local = jnp.einsum("nc,nd->cd", residual, proj_grad, preferred_element_type=f32)
    d_residual = (
        out_flat.astype(f32)
        + jnp.einsum("nd,cd->nc", proj_grad, qkv_weight, preferred_element_type=f32)
    ).astype(bf16)
    d_res_map = d_residual.reshape(samples, row_count, col_count, chan_count)
    d_padded = with_halo(d_res_map, (("dom", 1),), 1)
    d_padded = jnp.pad(d_padded, ((0, 0), (0, 0), (1, 1), (0, 0)))
    conv_parts = []
    d_act = jnp.zeros((samples * tok_count, chan_count), f32)
    for tap_index in range(9):
        row_off = tap_index // 3 - 1
        col_off = tap_index % 3 - 1
        conv_parts.append(
            jnp.einsum(
                "nc,nd->cd",
                shifted(padded, 1 + row_off, 1 + col_off),
                d_residual,
                preferred_element_type=f32,
            )
        )
        d_act = d_act + jnp.einsum(
            "nd,cd->nc",
            shifted(d_padded, 1 - row_off, 1 - col_off),
            conv_weight[tap_index],
            preferred_element_type=f32,
        )
    conv_local = jnp.stack(conv_parts)
    d_pre = (
        d_act.reshape(samples, row_count, col_count, chan_count)
        * sigmoid_pre
        * (1.0 + pre_act * (1.0 - sigmoid_pre))
    )
    gain_local = (d_pre * normed).sum((0, 1, 2))
    shift_local = d_pre.sum((0, 1, 2))
    scaled = d_pre * norm_gain
    scaled_groups = scaled.reshape(samples, row_count, col_count, GROUPS, group_width)
    product_groups = (scaled * normed).reshape(samples, row_count, col_count, GROUPS, group_width)
    back_sums = dom_psum(jnp.stack([scaled_groups.sum((1, 2, 4)), product_groups.sum((1, 2, 4))]))
    first = back_sums[0] / count
    second = back_sums[1] / count
    input_grad = (
        d_res_map.astype(f32)
        + per_channel(inv_std, group_width)
        * (scaled - per_channel(first, group_width) - normed * per_channel(second, group_width))
    ).astype(bf16)
    parts = (out_grad, qkv_local, conv_local, gain_local, shift_local)
    flat = jnp.concatenate([part.reshape(-1) for part in parts])
    total = flat.shape[0]
    padded_len = -(-total // 32768) * 32768
    flat = mesh_psum(jnp.pad(flat, (0, padded_len - total)))
    pieces = []
    offset = 0
    for part in parts:
        pieces.append(flat[offset : offset + part.size].reshape(part.shape))
        offset += part.size
    out_grad, qkv_grad, conv_grad, gain_grad, shift_grad = pieces
    return (input_grad, conv_grad, qkv_grad, out_grad, gain_grad, shift_grad)


def solution(mesh):
    placed = (
        P("batch", "dom", None, None),
        P("batch", "dom", None, None),
        P("batch", "dom", None, None),
        P("batch", "dom", None, None),
        P("batch", "dom", None, None),
        P("batch", "dom", None, None),
        P(),
        P(),
        P(),
        P(),
        P(),
    )
    return jax.shard_map(
        body,
        mesh=mesh,
        in_specs=placed,
        out_specs=(P("batch", "dom", None, None), P(), P(), P(), P(), P()),
        check_vma=False,
    )
```

profile of v0, /device:TPU:120, one launch (start us, length us, event | category | flops | bytes accessed | tf_op | source)
XLA Modules:
  0.0 436.7 jit_solution(5991941233304587757)
XLA Ops:
  9.3 1.9 copy.46
  17.9 2.8 collective-permute-done.5
  22.0 3.9 collective-permute-done.6
  25.9 1.5 collective-permute-start.7
  27.5 2.0 collective-permute-done.7
  29.5 21.2 %all-gather.5.cloned.1.call-done = bf16[2,4352,256]{2,1,0:T(8,128)(2,1)} async-done(((bf16[2,272,256]{2,1,0:T(8,128)(2,1)}), bf16[2,4352,256]{2,1,0:T(8,128)(2,1)}) %all-gather.5.cloned.1.call-update) | async-done | bytes 4456464 | tf_op jit(solution)/shard_map/all_gather | solution.py:177
  50.7 3.8 fusion.106
  56.0 2.2 copy-done.2
  59.1 33.8 %all-gather.7.cloned.1.call-done = bf16[2,4352,256]{2,0,1:T(2,128)(2,1)} async-done(((bf16[2,272,256]{2,0,1:T(2,128)(2,1)}), bf16[2,4352,256]{2,0,1:T(2,128)(2,1)}) %all-gather.7.cloned.1.call-update) | async-done | bytes 4456464 | tf_op jit(solution)/shard_map/all_gather | solution.py:178
  92.9 10.2 %fusion.19 = bf16[2,272,256]{2,1,0:T(8,128)(2,1)S(1)} fusion(bf16[2,4352,256]{2,1,0:T(8,128)(2,1)} %all-gather.5.cloned.1.call-done, f32[2,272,4352]{2,1,0:T(8,128)} %copy-done.2, bf16[2,272,256]{2,1,0:T(8,128)(2,1)S(1)} %bitcast.216, f32[2,272]{1,0:T(2,128)S(1)} %copy.64, f32[2,272]{1,0:T(2,128)S(1)} %log_add_fusion, ...), kind=kOutput, calls=%fused_computation.44 | convolution fusion | flops 2434056192 | bytes 18944256 | tf_op jit(solution)/shard_map/shqk,skhd->sqhd/dot_general | solution.py:183
  104.2 2.7 collective-permute-done.1
  107.0 2.2 collective-permute-start.2
  109.2 3.9 collective-permute-done.2
  113.9 4.5 %collective-permute-done.3 = f32[8,2,2,272,1]{3,0,2,4,1:T(8,128)S(1)} collective-permute-done((f32[8,2,2,272,1]{3,0,2,4,1:T(8,128)S(1)}, f32[8,2,2,272,1]{3,0,2,4,1:T(8,128)S(1)}, u32[]{:S(2)}, u32[]{:S(2)}) %collective-permute-start.3) | collective-permute-done | bytes 34848 | tf_op jit(solution)/shard_map/ppermute | solution.py:43
  118.7 17.1 %all-gather.9.cloned.1.call-done = bf16[2,4352,256]{2,1,0:T(8,128)(2,1)} async-done(((bf16[2,272,256]{2,1,0:T(8,128)(2,1)}), bf16[2,4352,256]{2,1,0:T(8,128)(2,1)}) %all-gather.9.cloned.1.call-update) | async-done | bytes 4456464 | tf_op jit(solution)/shard_map/all_gather | solution.py:187
  135.8 7.5 %subtract_exponential_fusion = f32[2,4352,272]{1,2,0:T(8,128)} fusion(bf16[2,4352,256]{2,1,0:T(8,128)(2,1)} %all-gather.9.cloned.1.call-done, f32[2,4352]{1,0:T(2,128)S(1)} %sub.118, bf16[2,272,256]{2,0,1:T(2,128)(2,1)S(1)} %bitcast.218), kind=kOutput, calls=%fused_computation.1 | convolution fusion | flops 1216888832 | bytes 14239744 | tf_op jit(solution)/shard_map/sqhd,skhd->shqk/dot_general | solution.py:143
  143.3 34.9 %all-gather.11.cloned.1.call-done = bf16[2,4352,256]{2,1,0:T(8,128)(2,1)} async-done(((bf16[2,272,256]{2,1,0:T(8,128)(2,1)}), bf16[2,4352,256]{2,1,0:T(8,128)(2,1)}) %all-gather.11.cloned.1.call-update) | async-done | bytes 4456464 | tf_op jit(solution)/shard_map/all_gather | solution.py:188
  178.1 6.3 %fusion.14 = bf16[2,256,272]{1,2,0:T(8,128)(2,1)S(1)} fusion(bf16[2,4352,256]{2,1,0:T(8,128)(2,1)} %all-gather.11.cloned.1.call-done, f32[2,4352,272]{1,2,0:T(8,128)} %subtract_exponential_fusion), kind=kOutput, calls=%fused_computation.40 | convolution fusion | flops 1214660608 | bytes 14204928 | tf_op jit(solution)/shard_map/shqk,sqhd->skhd/dot_general | solution.py:196
  184.5 9.0 %fusion.13 = bf16[2,272,256]{2,1,0:T(8,128)(2,1)S(1)} fusion(bf16[2,4352,256]{2,1,0:T(8,128)(2,1)} %all-gather.9.cloned.1.call-done, f32[2,4352,272]{1,2,0:T(8,128)} %subtract_exponential_fusion, bf16[2,4352,256]{2,1,0:T(8,128)(2,1)} %all-gather.11.cloned.1.call-done, f32[2,4352]{1,0:T(2,128)S(1)} %sub.121, bf16[2,272,256]{2,0,1:T(2,128)(2,1)S(1)} %bitcast.220), kind=kOutput, calls=%fused_computation.39 | convolution fusion | flops 2431688704 | bytes 18974720 | tf_op jit(solution)/shard_map/shqk,sqhd->skhd/dot_general | solution.py:195
  194.0 2.1 collective-permute-start.8
  196.1 3.6 collective-permute-start.9
  204.3 1.7 reshape.731
  206.0 1.7 reshape.730
  217.5 1.9 multiply_reduce_fusion
  219.3 6.3 %collective-permute-start.14 = (bf16[2,1,68,256]{3,2,1,0:T(8,128)(2,1)S(1)}, bf16[2,1,68,256]{3,2,1,0:T(8,128)(2,1)S(1)}, u32[]{:S(2)}, u32[]{:S(2)}) collective-permute-start(bf16[2,1,68,256]{3,2,1,0:T(8,128)(2,1)S(1)} %get-tuple-element.41), channel_id=1, source_target_pairs={{0,1},{1,2},{2,3},{3,4},{4,5},{5,6},{6,7},{7,8},{8,9},{9,10},{10,1... | collective-permute-start | bytes 208904 | tf_op jit(solution)/shard_map/ppermute | solution.py:19
  225.6 1.9 collective-permute-start.15
  236.8 2.1 convolution_add_fusion.7
  244.4 3.0 fusion.22
  248.7 2.0 fusion.30
  257.8 3.0 copy.67
  261.8 1.5 fusion.6
  264.1 3.9 collective-permute-start.16
  268.1 3.7 collective-permute-done.16
  271.7 2.2 select_add_fusion
  275.4 13.0 %collective-permute-done.17 = f32[221184]{0:T(1024)S(1)} collective-permute-done((f32[221184]{0:T(1024)S(1)}, f32[221184]{0:T(1024)S(1)}, u32[]{:S(2)}, u32[]{:S(2)}) %collective-permute-start.17) | collective-permute-done | bytes 884768 | tf_op jit(solution)/shard_map/ppermute | solution.py:71
  288.4 1.6 select_add_fusion.1
  290.1 8.3 %collective-permute-done.18 = f32[110592]{0:T(1024)S(1)} collective-permute-done((f32[110592]{0:T(1024)S(1)}, f32[110592]{0:T(1024)S(1)}, u32[]{:S(2)}, u32[]{:S(2)}) %collective-permute-start.18) | collective-permute-done | bytes 442400 | tf_op jit(solution)/shard_map/ppermute | solution.py:71
  299.3 5.5 %collective-permute-done.19 = f32[55296]{0:T(1024)S(1)} collective-permute-done((f32[55296]{0:T(1024)S(1)}, f32[55296]{0:T(1024)S(1)}, u32[]{:S(2)}, u32[]{:S(2)}) %collective-permute-start.19) | collective-permute-done | bytes 221216 | tf_op jit(solution)/shard_map/ppermute | solution.py:71
  304.9 6.2 %collective-permute-done.20 = f32[27648]{0:T(1024)S(1)} collective-permute-done((f32[27648]{0:T(1024)S(1)}, f32[27648]{0:T(1024)S(1)}, u32[]{:S(2)}, u32[]{:S(2)}) %collective-permute-start.20) | collective-permute-done | bytes 110624 | tf_op jit(solution)/shard_map/ppermute | solution.py:71
  311.2 2.8 collective-permute-start.21
  314.0 3.0 collective-permute-done.21
  317.7 4.4 %collective-permute-done.22 = f32[6912]{0:T(1024)S(1)} collective-permute-done((f32[6912]{0:T(1024)S(1)}, f32[6912]{0:T(1024)S(1)}, u32[]{:S(2)}, u32[]{:S(2)}) %collective-permute-start.22) | collective-permute-done | bytes 27680 | tf_op jit(solution)/shard_map/ppermute | solution.py:71
  322.2 2.8 collective-permute-start.23
  325.0 4.9 %collective-permute-done.23 = f32[3456]{0:T(1024)S(1)} collective-permute-done((f32[3456]{0:T(1024)S(1)}, f32[3456]{0:T(1024)S(1)}, u32[]{:S(2)}, u32[]{:S(2)}) %collective-permute-start.23) | collective-permute-done | bytes 13856 | tf_op jit(solution)/shard_map/ppermute | solution.py:71
  329.9 2.7 collective-permute-start.24
  332.6 4.9 %collective-permute-done.24 = f32[3456]{0:T(1024)S(1)} collective-permute-done((f32[3456]{0:T(1024)S(1)}, f32[3456]{0:T(1024)S(1)}, u32[]{:S(2)}, u32[]{:S(2)}) %collective-permute-start.24) | collective-permute-done | bytes 13856 | tf_op jit(solution)/shard_map/ppermute | solution.py:74
  338.0 6.0 %collective-permute-done.25 = f32[6912]{0:T(1024)S(1)} collective-permute-done((f32[6912]{0:T(1024)S(1)}, f32[6912]{0:T(1024)S(1)}, u32[]{:S(2)}, u32[]{:S(2)}) %collective-permute-start.25) | collective-permute-done | bytes 27680 | tf_op jit(solution)/shard_map/ppermute | solution.py:74
  344.0 2.8 collective-permute-start.26
  346.8 3.6 collective-permute-done.26
  350.5 7.4 %collective-permute-done.27 = f32[27648]{0:T(1024)S(1)} collective-permute-done((f32[27648]{0:T(1024)S(1)}, f32[27648]{0:T(1024)S(1)}, u32[]{:S(2)}, u32[]{:S(2)}) %collective-permute-start.27) | collective-permute-done | bytes 110624 | tf_op jit(solution)/shard_map/ppermute | solution.py:74
  358.0 8.3 %collective-permute-done.28 = f32[55296]{0:T(1024)S(1)} collective-permute-done((f32[55296]{0:T(1024)S(1)}, f32[55296]{0:T(1024)S(1)}, u32[]{:S(2)}, u32[]{:S(2)}) %collective-permute-start.28) | collective-permute-done | bytes 221216 | tf_op jit(solution)/shard_map/ppermute | solution.py:74
  367.0 7.8 %collective-permute-done.29 = f32[110592]{0:T(1024)S(1)} collective-permute-done((f32[110592]{0:T(1024)S(1)}, f32[110592]{0:T(1024)S(1)}, u32[]{:S(2)}, u32[]{:S(2)}) %collective-permute-start.29) | collective-permute-done | bytes 442400 | tf_op jit(solution)/shard_map/ppermute | solution.py:74
  375.5 13.0 %collective-permute-done.30 = f32[221184]{0:T(1024)S(1)} collective-permute-done((f32[221184]{0:T(1024)S(1)}, f32[221184]{0:T(1024)S(1)}, u32[]{:S(2)}, u32[]{:S(2)}) %collective-permute-start.30) | collective-permute-done | bytes 884768 | tf_op jit(solution)/shard_map/ppermute | solution.py:74
  391.0 2.9 collective-permute-done.10
  393.9 3.6 collective-permute-done.11
  397.5 5.1 %collective-permute-done.12 = f32[2,2,32]{2,1,0:T(2,128)S(1)} collective-permute-done((f32[2,2,32]{2,1,0:T(2,128)S(1)}, f32[2,2,32]{2,1,0:T(2,128)S(1)}, u32[]{:S(2)}, u32[]{:S(2)}) %collective-permute-start.12) | collective-permute-done | bytes 544 | tf_op jit(solution)/shard_map/ppermute | solution.py:32
  402.8 3.6 collective-permute-done.13
  410.7 1.9 concatenate.347
  412.7 2.5 maximum_select_fusion.4
  416.3 3.5 maximum_select_fusion.2
  419.7 3.0 maximum_select_fusion
  423.6 1.8 reshape.748
  426.3 1.8 concatenate.345
  428.2 1.7 fusion.37
  (266 shorter events, 69.1 us)
Async XLA Ops:
  7.2 186.3 %copy-start = (bf16[256,768]{1,0:T(8,128)(2,1)S(1)}, bf16[256,768]{1,0:T(8,128)(2,1)}, u32[]{:S(2)}) copy-start(bf16[256,768]{1,0:T(8,128)(2,1)} %param.18) | copy-start | bytes 1179652
  7.2 4.2 copy-start.30
  7.2 5.2 %copy-start.31 = (bf16[2,4,68,256]{3,1,2,0:T(4,128)(2,1)S(1)}, bf16[2,4,68,256]{3,1,2,0:T(4,128)(2,1)}, u32[]{:S(2)}) copy-start(bf16[2,4,68,256]{3,1,2,0:T(4,128)(2,1)} %param.16) | copy-start | bytes 835588
  7.2 5.3 %copy-start.35 = (bf16[256,256]{1,0:T(8,128)(2,1)S(1)}, bf16[256,256]{1,0:T(8,128)(2,1)}, u32[]{:S(2)}) copy-start(bf16[256,256]{1,0:T(8,128)(2,1)} %param.19) | copy-start | bytes 393220
  7.2 43.5 %all-gather.5.cloned.1.call-start = ((), (), s32[]{:S(2)}) async-start(), calls=%async_computation | async-start | bytes 4734976 | tf_op jit(solution)/shard_map/all_gather | solution.py:177
  9.2 4.3 copy-start.7
  9.3 83.6 %all-gather.7.cloned.1.call-start = ((), (), s32[]{:S(2)}) async-start(), calls=%async_computation.1 | async-start | bytes 4734976 | tf_op jit(solution)/shard_map/all_gather | solution.py:178
  11.3 3.9 copy-start.32
  11.3 124.5 %all-gather.9.cloned.1.call-start = ((), (), s32[]{:S(2)}) async-start(), calls=%async_computation.2 | async-start | bytes 4734976 | tf_op jit(solution)/shard_map/all_gather | solution.py:187
  12.3 165.8 %all-gather.11.cloned.1.call-start = ((), (), s32[]{:S(2)}) async-start(), calls=%async_computation.3 | async-start | bytes 4734976 | tf_op jit(solution)/shard_map/all_gather | solution.py:188
  14.0 3.1 collective-permute-start.4
  15.8 38.7 %copy-start.10 = (f32[32,2,8,128]{3,1,2,0:T(2,128)}, f32[32,2,8,128]{3,1,2,0:T(2,128)S(1)}, u32[]{:S(2)}) copy-start(f32[32,2,8,128]{3,1,2,0:T(2,128)S(1)} %copy.66) | copy-start | bytes 786436
  17.1 3.7 collective-permute-start.5
  20.8 5.1 %collective-permute-start.6 = (f32[2,2,32]{2,1,0:T(2,128)S(1)}, f32[2,2,32]{2,1,0:T(2,128)S(1)}, u32[]{:S(2)}, u32[]{:S(2)}) collective-permute-start(f32[2,2,32]{2,1,0:T(2,128)S(1)} %fusion.154), channel_id=1, source_target_pairs={{0,4},{1,5},{2,6},{3,7},{4,0},{5,1},{6,2},{7,3},{8,12},{9,13},{10,... | collective-permute-start | bytes 1544 | tf_op jit(solution)/shard_map/ppermute | solution.py:32
  25.9 3.6 collective-permute-start.7
  54.5 3.7 copy-start.2
  54.6 38.3 %copy-start.12 = (bf16[544,256]{1,0:T(8,128)(2,1)S(1)}, bf16[544,256]{1,0:T(8,128)(2,1)}, u32[]{:S(2)}) copy-start(bf16[544,256]{1,0:T(8,128)(2,1)} %convolution_convert_fusion) | copy-start | bytes 835588
  58.3 44.9 %collective-permute-start = (f32[1,2,2,272,1]{3,4,2,1,0:T(1,128)S(1)}, f32[1,2,2,272,1]{3,4,2,1,0:T(1,128)S(1)}, u32[]{:S(2)}, u32[]{:S(2)}) collective-permute-start(f32[1,2,2,272,1]{3,4,2,1,0:T(1,128)S(1)} %get-tuple-element.50), channel_id=1, source_target_pairs={{0,1},{1,0},{2,3},{3,2},{4,5},{5,4},{6,7},{7,6},{8,9},{9,8},{10,11... | collective-permute-start | bytes 13064 | tf_op jit(solution)/shard_map/ppermute | solution.py:43
  103.1 90.4 %copy-start.40 = (bf16[2,272,256]{2,1,0:T(8,128)(2,1)}, bf16[2,272,256]{2,1,0:T(8,128)(2,1)S(1)}, u32[]{:S(2)}) copy-start(bf16[2,272,256]{2,1,0:T(8,128)(2,1)S(1)} %fusion.19) | copy-start | bytes 835588
  103.2 3.8 collective-permute-start.1
  107.0 6.1 %collective-permute-start.2 = (f32[4,2,2,272,1]{3,0,2,1,4:T(4,128)S(1)}, f32[4,2,2,272,1]{3,0,2,1,4:T(4,128)S(1)}, u32[]{:S(2)}, u32[]{:S(2)}) collective-permute-start(f32[4,2,2,272,1]{3,0,2,1,4:T(4,128)S(1)} %maximum_select_fusion.14), channel_id=1, source_target_pairs={{0,4},{1,5},{2,6},{3,7},{4,0},{5,1},{6,2},{7,3},{8,12},{9,13},{10,... | collective-permute-start | bytes 52232 | tf_op jit(solution)/shard_map/ppermute | solution.py:43
  113.1 5.3 %collective-permute-start.3 = (f32[8,2,2,272,1]{3,0,2,4,1:T(8,128)S(1)}, f32[8,2,2,272,1]{3,0,2,4,1:T(8,128)S(1)}, u32[]{:S(2)}, u32[]{:S(2)}) collective-permute-start(f32[8,2,2,272,1]{3,0,2,4,1:T(8,128)S(1)} %fusion.81), channel_id=1, source_target_pairs={{0,8},{1,9},{2,10},{3,11},{4,12},{5,13},{6,14},{7,15},{8,0},{9,1},... | collective-permute-start | bytes 104456 | tf_op jit(solution)/shard_map/ppermute | solution.py:43
  143.3 41.2 %copy-start.19 = (bf16[2,4,68,256]{3,0,2,1:T(2,128)(2,1)S(1)}, bf16[2,4,68,256]{3,0,2,1:T(2,128)(2,1)}, u32[]{:S(2)}) copy-start(bf16[2,4,68,256]{3,0,2,1:T(2,128)(2,1)} %copy.46) | copy-start | bytes 835588
  184.5 9.0 %copy-start.28 = (bf16[2,256,272]{1,2,0:T(8,128)(2,1)}, bf16[2,256,272]{1,2,0:T(8,128)(2,1)S(1)}, u32[]{:S(2)}) copy-start(bf16[2,256,272]{1,2,0:T(8,128)(2,1)S(1)} %fusion.14) | copy-start | bytes 835588
  193.5 8.1 %copy-start.33 = (bf16[2,272,256]{2,1,0:T(8,128)(2,1)}, bf16[2,272,256]{2,1,0:T(8,128)(2,1)S(1)}, u32[]{:S(2)}) copy-start(bf16[2,272,256]{2,1,0:T(8,128)(2,1)S(1)} %fusion.13) | copy-start | bytes 835588
  194.0 6.1 %collective-permute-start.8 = (bf16[2,1,68,256]{3,2,1,0:T(8,128)(2,1)S(1)}, bf16[2,1,68,256]{3,2,1,0:T(8,128)(2,1)S(1)}, u32[]{:S(2)}, u32[]{:S(2)}) collective-permute-start(bf16[2,1,68,256]{3,2,1,0:T(8,128)(2,1)S(1)} %get-tuple-element.45), channel_id=1, source_target_pairs={{0,1},{1,2},{2,3},{3,4},{4,5},{5,6},{6,7},{7,8},{8,9},{9,10},{10,1... | collective-permute-start | bytes 208904 | tf_op jit(solution)/shard_map/ppermute | solution.py:19
  196.1 5.4 %collective-permute-start.9 = (bf16[2,1,68,256]{3,2,1,0:T(8,128)(2,1)S(1)}, bf16[2,1,68,256]{3,2,1,0:T(8,128)(2,1)S(1)}, u32[]{:S(2)}, u32[]{:S(2)}) collective-permute-start(bf16[2,1,68,256]{3,2,1,0:T(8,128)(2,1)S(1)} %get-tuple-element.46), channel_id=1, source_target_pairs={{1,0},{2,1},{3,2},{4,3},{5,4},{6,5},{7,6},{8,7},{9,8},{10,9},{11,1... | collective-permute-start | bytes 208904 | tf_op jit(solution)/shard_map/ppermute | solution.py:21
  203.3 6.0 %copy-start.9 = (bf16[9,256,256]{2,1,0:T(8,128)(2,1)S(1)}, bf16[9,256,256]{2,1,0:T(8,128)(2,1)}, u32[]{:S(2)}) copy-start(bf16[9,256,256]{2,1,0:T(8,128)(2,1)} %param.17) | copy-start | bytes 3538948
  208.6 3.5 copy-start.25
  219.3 9.2 %collective-permute-start.14 = (bf16[2,1,68,256]{3,2,1,0:T(8,128)(2,1)S(1)}, bf16[2,1,68,256]{3,2,1,0:T(8,128)(2,1)S(1)}, u32[]{:S(2)}, u32[]{:S(2)}) collective-permute-start(bf16[2,1,68,256]{3,2,1,0:T(8,128)(2,1)S(1)} %get-tuple-element.41), channel_id=1, source_target_pairs={{0,1},{1,2},{2,3},{3,4},{4,5},{5,6},{6,7},{7,8},{8,9},{9,10},{10,1... | collective-permute-start | bytes 208904 | tf_op jit(solution)/shard_map/ppermute | solution.py:19
  225.6 3.9 collective-permute-start.15
  233.5 9.1 %copy-start.15 = (bf16[544,256]{1,0:T(8,128)(2,1)}, bf16[544,256]{1,0:T(8,128)(2,1)S(1)}, u32[]{:S(2)}) copy-start(bf16[544,256]{1,0:T(8,128)(2,1)S(1)} %reshape.740) | copy-start | bytes 835588
  234.6 6.5 %copy-start.17 = (bf16[544,256]{1,0:T(8,128)(2,1)}, bf16[544,256]{1,0:T(8,128)(2,1)S(1)}, u32[]{:S(2)}) copy-start(bf16[544,256]{1,0:T(8,128)(2,1)S(1)} %reshape.739) | copy-start | bytes 835588
  239.9 3.0 copy-start.13
  247.4 3.3 copy-start.18
  247.4 4.3 copy-start.16
  248.7 7.1 %copy-start.22 = (bf16[544,256]{1,0:T(8,128)(2,1)S(1)}, bf16[544,256]{1,0:T(8,128)(2,1)}, u32[]{:S(2)}) copy-start(bf16[544,256]{1,0:T(8,128)(2,1)} %reshape.744) | copy-start | bytes 835588
  250.7 6.1 %copy-start.14 = (bf16[544,256]{1,0:T(8,128)(2,1)S(1)}, bf16[544,256]{1,0:T(8,128)(2,1)}, u32[]{:S(2)}) copy-start(bf16[544,256]{1,0:T(8,128)(2,1)} %copy-done.13) | copy-start | bytes 835588
  257.8 3.0 copy-start.4
  264.1 7.6 %collective-permute-start.16 = (f32[442368]{0:T(1024)}, f32[442368]{0:T(1024)}, u32[]{:S(2)}, u32[]{:S(2)}) collective-permute-start(f32[442368]{0:T(1024)} %fusion.6), channel_id=1, source_target_pairs={{0,1},{1,0},{2,3},{3,2},{4,5},{5,4},{6,7},{7,6},{8,9},{9,8},{10,11... | collective-permute-start | bytes 5308424 | tf_op jit(solution)/shard_map/ppermute | solution.py:71
  275.3 13.1 %collective-permute-start.17 = (f32[221184]{0:T(1024)S(1)}, f32[221184]{0:T(1024)S(1)}, u32[]{:S(2)}, u32[]{:S(2)}) collective-permute-start(f32[221184]{0:T(1024)S(1)} %slice_select_fusion), channel_id=1, source_target_pairs={{0,2},{1,17},{2,0},{3,19},{4,6},{5,21},{6,4},{7,23},{8,10},{9,25},... | collective-permute-start | bytes 2654216 | tf_op jit(solution)/shard_map/ppermute | solution.py:71
  290.0 8.4 %collective-permute-start.18 = (f32[110592]{0:T(1024)S(1)}, f32[110592]{0:T(1024)S(1)}, u32[]{:S(2)}, u32[]{:S(2)}) collective-permute-start(f32[110592]{0:T(1024)S(1)} %slice_select_fusion.1), channel_id=1, source_target_pairs={{0,8},{1,3},{2,10},{3,1},{4,12},{5,7},{6,14},{7,5},{8,0},{9,11},{1... | collective-permute-start | bytes 1327112 | tf_op jit(solution)/shard_map/ppermute | solution.py:71
  298.5 6.2 %collective-permute-start.19 = (f32[55296]{0:T(1024)S(1)}, f32[55296]{0:T(1024)S(1)}, u32[]{:S(2)}, u32[]{:S(2)}) collective-permute-start(f32[55296]{0:T(1024)S(1)} %slice_select_fusion.2), channel_id=1, source_target_pairs={{0,16},{1,9},{2,18},{3,11},{4,20},{5,13},{6,22},{7,15},{8,24},{9,1... | collective-permute-start | bytes 663560 | tf_op jit(solution)/shard_map/ppermute | solution.py:71
  304.8 6.3 %collective-permute-start.20 = (f32[27648]{0:T(1024)S(1)}, f32[27648]{0:T(1024)S(1)}, u32[]{:S(2)}, u32[]{:S(2)}) collective-permute-start(f32[27648]{0:T(1024)S(1)} %slice_select_fusion.3), channel_id=1, source_target_pairs={{0,4},{1,33},{2,6},{3,35},{4,0},{5,37},{6,2},{7,39},{8,12},{9,41},... | collective-permute-start | bytes 331784 | tf_op jit(solution)/shard_map/ppermute | solution.py:71
  311.2 5.8 %collective-permute-start.21 = (f32[13824]{0:T(1024)S(1)}, f32[13824]{0:T(1024)S(1)}, u32[]{:S(2)}, u32[]{:S(2)}) collective-permute-start(f32[13824]{0:T(1024)S(1)} %slice_select_fusion.4), channel_id=1, source_target_pairs={{0,128},{1,5},{2,130},{3,7},{4,132},{5,1},{6,134},{7,3},{8,136},{9... | collective-permute-start | bytes 165896 | tf_op jit(solution)/shard_map/ppermute | solution.py:71
  317.0 5.2 %collective-permute-start.22 = (f32[6912]{0:T(1024)S(1)}, f32[6912]{0:T(1024)S(1)}, u32[]{:S(2)}, u32[]{:S(2)}) collective-permute-start(f32[6912]{0:T(1024)S(1)} %slice_select_fusion.5), channel_id=1, source_target_pairs={{0,32},{1,129},{2,34},{3,131},{4,36},{5,133},{6,38},{7,135},{8,40}... | collective-permute-start | bytes 82952 | tf_op jit(solution)/shard_map/ppermute | solution.py:71
  322.2 7.7 %collective-permute-start.23 = (f32[3456]{0:T(1024)S(1)}, f32[3456]{0:T(1024)S(1)}, u32[]{:S(2)}, u32[]{:S(2)}) collective-permute-start(f32[3456]{0:T(1024)S(1)} %slice_select_fusion.6), channel_id=1, source_target_pairs={{0,64},{1,65},{2,66},{3,67},{4,68},{5,69},{6,70},{7,71},{8,72},{9,... | collective-permute-start | bytes 41480 | tf_op jit(solution)/shard_map/ppermute | solution.py:71
  329.9 7.6 %collective-permute-start.24 = (f32[3456]{0:T(1024)S(1)}, f32[3456]{0:T(1024)S(1)}, u32[]{:S(2)}, u32[]{:S(2)}) collective-permute-start(f32[3456]{0:T(1024)S(1)} %select_add_fusion.7), channel_id=1, source_target_pairs={{0,64},{1,65},{2,66},{3,67},{4,68},{5,69},{6,70},{7,71},{8,72},{9,... | collective-permute-start | bytes 41480 | tf_op jit(solution)/shard_map/ppermute | solution.py:74
  337.6 6.4 %collective-permute-start.25 = (f32[6912]{0:T(1024)S(1)}, f32[6912]{0:T(1024)S(1)}, u32[]{:S(2)}, u32[]{:S(2)}) collective-permute-start(f32[6912]{0:T(1024)S(1)} %maximum_select_fusion.13), channel_id=1, source_target_pairs={{0,32},{1,129},{2,34},{3,131},{4,36},{5,133},{6,38},{7,135},{8,40}... | collective-permute-start | bytes 82952 | tf_op jit(solution)/shard_map/ppermute | solution.py:74
  344.0 6.4 %collective-permute-start.26 = (f32[13824]{0:T(1024)S(1)}, f32[13824]{0:T(1024)S(1)}, u32[]{:S(2)}, u32[]{:S(2)}) collective-permute-start(f32[13824]{0:T(1024)S(1)} %maximum_select_fusion.10), channel_id=1, source_target_pairs={{0,128},{1,5},{2,130},{3,7},{4,132},{5,1},{6,134},{7,3},{8,136},{9... | collective-permute-start | bytes 165896 | tf_op jit(solution)/shard_map/ppermute | solution.py:74
  350.4 7.5 %collective-permute-start.27 = (f32[27648]{0:T(1024)S(1)}, f32[27648]{0:T(1024)S(1)}, u32[]{:S(2)}, u32[]{:S(2)}) collective-permute-start(f32[27648]{0:T(1024)S(1)} %maximum_select_fusion.8), channel_id=1, source_target_pairs={{0,4},{1,33},{2,6},{3,35},{4,0},{5,37},{6,2},{7,39},{8,12},{9,41},... | collective-permute-start | bytes 331784 | tf_op jit(solution)/shard_map/ppermute | solution.py:74
  357.9 8.4 %collective-permute-start.28 = (f32[55296]{0:T(1024)S(1)}, f32[55296]{0:T(1024)S(1)}, u32[]{:S(2)}, u32[]{:S(2)}) collective-permute-start(f32[55296]{0:T(1024)S(1)} %maximum_select_fusion.7), channel_id=1, source_target_pairs={{0,16},{1,9},{2,18},{3,11},{4,20},{5,13},{6,22},{7,15},{8,24},{9,1... | collective-permute-start | bytes 663560 | tf_op jit(solution)/shard_map/ppermute | solution.py:74
  366.4 23.8 %copy-start.36 = (f32[2,256]{1,0:T(2,128)S(1)}, f32[2,256]{1,0:T(2,128)}, u32[]{:S(2)}) copy-start(f32[2,256]{1,0:T(2,128)} %get-tuple-element.20) | copy-start | bytes 6148
  366.4 8.4 %collective-permute-start.29 = (f32[110592]{0:T(1024)S(1)}, f32[110592]{0:T(1024)S(1)}, u32[]{:S(2)}, u32[]{:S(2)}) collective-permute-start(f32[110592]{0:T(1024)S(1)} %maximum_select_fusion.5), channel_id=1, source_target_pairs={{0,8},{1,3},{2,10},{3,1},{4,12},{5,7},{6,14},{7,5},{8,0},{9,11},{1... | collective-permute-start | bytes 1327112 | tf_op jit(solution)/shard_map/ppermute | solution.py:74
  375.5 31.2 %copy-start.8 = (bf16[2,4,68,256]{3,1,2,0:T(4,128)(2,1)S(1)}, bf16[2,4,68,256]{3,1,2,0:T(4,128)(2,1)}, u32[]{:S(2)}) copy-start(bf16[2,4,68,256]{3,1,2,0:T(4,128)(2,1)} %param.11) | copy-start | bytes 835588
  375.5 31.2 %copy-start.38 = (f32[256]{0:T(256)S(1)}, f32[256]{0:T(256)}, u32[]{:S(2)}) copy-start(f32[256]{0:T(256)} %param.20) | copy-start | bytes 3076
  375.5 13.0 %collective-permute-start.30 = (f32[221184]{0:T(1024)S(1)}, f32[221184]{0:T(1024)S(1)}, u32[]{:S(2)}, u32[]{:S(2)}) collective-permute-start(f32[221184]{0:T(1024)S(1)} %maximum_select_fusion.3), channel_id=1, source_target_pairs={{0,2},{1,17},{2,0},{3,19},{4,6},{5,21},{6,4},{7,23},{8,10},{9,25},... | collective-permute-start | bytes 2654216 | tf_op jit(solution)/shard_map/ppermute | solution.py:74
  390.0 29.8 %collective-permute-start.31 = (f32[442368]{0:T(1024)}, f32[442368]{0:T(1024)S(1)}, u32[]{:S(2)}, u32[]{:S(2)}) collective-permute-start(f32[442368]{0:T(1024)} %maximum_select_fusion.1), channel_id=1, source_target_pairs={{0,1},{1,0},{2,3},{3,2},{4,5},{5,4},{6,7},{7,6},{8,9},{9,8},{10,11... | collective-permute-start | bytes 5308424 | tf_op jit(solution)/shard_map/ppermute | solution.py:74
  390.4 3.5 collective-permute-start.10
  393.9 3.6 collective-permute-start.11
  397.5 5.1 %collective-permute-start.12 = (f32[2,2,32]{2,1,0:T(2,128)S(1)}, f32[2,2,32]{2,1,0:T(2,128)S(1)}, u32[]{:S(2)}, u32[]{:S(2)}) collective-permute-start(f32[2,2,32]{2,1,0:T(2,128)S(1)} %fusion.153), channel_id=1, source_target_pairs={{0,4},{1,5},{2,6},{3,7},{4,0},{5,1},{6,2},{7,3},{8,12},{9,13},{10,... | collective-permute-start | bytes 1544 | tf_op jit(solution)/shard_map/ppermute | solution.py:32
  402.6 3.8 collective-permute-start.13
  419.7 3.0 copy-start.6
  426.3 3.5 copy-start.1
  (13 other events, 22.4 us)
Sparse Core Ops, SparseCore 0:
  10.4 40.2 all-gather.4
  52.6 40.2 all-gather.6
  95.3 40.4 all-gather.8
  138.0 40.0 all-gather.10
where the time goes:
time: 444 us; the launch traced here: 437 us
  waiting for transfers between devices  244 us (55%)
  matrix products  64.2 us (14%)
  local copies, waits for them, and re-layouts  46 us (10%)
  starting transfers between devices  40.9 us (9%)
  other arithmetic  26 us (6%)
  between operations  15.3 us (3%)
    ppermute x8, waiting for transfers between devices, mesh_psum(): got = lax.ppermute(values, MESH_AXES, pairs)  51 us
    ppermute x8, waiting for transfers between devices, mesh_psum(): values = keep + lax.ppermute(send, MESH_AXES, pairs)  49 us
    all_gather x1, waiting for transfers between devices, body(): lax.all_gather(do_rows, 'dom', axis=1, tiled=True)  34.9 us
    all_gather x1, waiting for transfers between devices, body(): lax.all_gather(v_rows, 'dom', axis=1, tiled=True)  33.8 us
    ppermute x8, waiting for transfers between devices, dom_psum(): lax.ppermute(values, 'dom', [(i, i ^ step) for i in range(count)])  23.9 us
    all_gather x1, waiting for transfers between devices, body(): lax.all_gather(k_rows, 'dom', axis=1, tiled=True)  21.2 us
    all_gather x1, waiting for transfers between devices, body(): lax.all_gather(q_rows, 'dom', axis=1, tiled=True)  17.1 us
    unnamed x94, local copies, waits for them, and re-layouts  14.9 us
  transfers between devices with their start and end apart: 36, of which 31 were waited for; matrix products, arithmetic and copies ran while one was open for 10% of the time, Pallas kernels for 0%

commit v1 on v0

--- a/solution.py
+++ b/solution.py
@@ -185,7 +185,9 @@
     stats_all = stats_local.transpose(1, 2, 0, 3, 4).reshape(2, samples, -1, HEADS)
     shard_piece = (
         lax.all_gather(q_rows, "dom", axis=1, tiled=True),
-        lax.all_gather(do_rows, "dom", axis=1, tiled=True),
+        jnp.concatenate(
+            lax.all_to_all(jnp.stack([do_rows] * lax.axis_size("dom")), "dom", 0, 0), axis=1
+        ),
     )
     query_heads = split_heads(shard_piece[0])
     dout_heads = split_heads(shard_piece[1])

time: 444 us -> 457 us (1.029)
  local copies, waits for them, and re-layouts: 46 us -> 56.9 us
  matrix products: 64.2 us -> 57 us
  waiting for transfers between devices: 244 us -> 251 us
    ppermute x8, waiting for transfers between devices: 23.9 us -> 94.1 us  [dom_psum(): lax.ppermute(values, 'dom', [(i, i ^ step) for i in range(count)])]
    all_gather x1 -> x0, waiting for transfers between devices: 34.9 us -> none  [body(): lax.all_gather(do_rows, 'dom', axis=1, tiled=True)]
    all_gather x1, waiting for transfers between devices: 21.2 us -> 0.01 us  [body(): lax.all_gather(k_rows, 'dom', axis=1, tiled=True)]
    all_gather x1, waiting for transfers between devices: 33.8 us -> 25.7 us  [body(): lax.all_gather(v_rows, 'dom', axis=1, tiled=True)]
    all_to_all x0 -> x1, starting transfers between devices: none -> 5.76 us  [body(): lax.all_to_all(jnp.stack([do_rows] * lax.axis_size('dom')), 'dom', 0, 0)]
    reshape x1 -> x2, local copies, waits for them, and re-layouts: 0.74 us -> 5.45 us  [the longest x1 4.71 us: body(): jnp.concatenate(lax.all_to_all(jnp.stack([do_rows] * lax.axis_size('dom')...]
  transfers between devices with their start and end apart: 36 -> 36, of which waited for: 31 -> 29; matrix products, arithmetic and copies ran while one was open for 10% -> 10% of each run, Pallas kernels for 0% -> 0%
where the time goes in v1:
time: 457 us; the launch traced here: 449 us
  waiting for transfers between devices  251 us (55%)
  matrix products  57 us (12%)
  local copies, waits for them, and re-layouts  56.9 us (12%)
  starting transfers between devices  44.5 us (10%)
  other arithmetic  25 us (5%)
  between operations  15.2 us (3%)
    ppermute x8, waiting for transfers between devices, dom_psum(): lax.ppermute(values, 'dom', [(i, i ^ step) for i in range(count)])  94.1 us
    ppermute x8, waiting for transfers between devices, mesh_psum(): got = lax.ppermute(values, MESH_AXES, pairs)  51 us
    ppermute x8, waiting for transfers between devices, mesh_psum(): values = keep + lax.ppermute(send, MESH_AXES, pairs)  49 us
    all_gather x1, waiting for transfers between devices, body(): lax.all_gather(v_rows, 'dom', axis=1, tiled=True)  25.7 us
    unnamed x94, local copies, waits for them, and re-layouts  18.5 us
    all_gather x1, waiting for transfers between devices, body(): lax.all_gather(q_rows, 'dom', axis=1, tiled=True)  17.4 us
    reshape x17, local copies, waits for them, and re-layouts, shifted(): return source[:, row_start:row_start + row_count, col_start:col_start + c...  13.3 us
    select_n x12, other arithmetic, mesh_psum(): jnp.where(upper, jnp.concatenate([got, values]), jnp.concatenate([values,...  13 us
  transfers between devices with their start and end apart: 36, of which 29 were waited for; matrix products, arithmetic and copies ran while one was open for 10% of the time, Pallas kernels for 0%

profile of v1, /device:TPU:120, one launch (start us, length us, event | category | flops | bytes accessed | tf_op | source)
XLA Modules:
  0.0 449.3 jit_solution(17334134595304503945)
XLA Ops:
  9.3 1.9 copy.46
  12.7 2.6 stack.59
  15.2 5.8 %all-to-all-start = ((bf16[16,2,272,256]{3,2,1,0:T(8,128)(2,1)}), bf16[16,2,272,256]{3,2,1,0:T(8,128)(2,1)}, u32[]{:S(2)}, u32[]{:S(2)}) async-start(bf16[16,2,272,256]{3,2,1,0:T(8,128)(2,1)} %stack.59), calls=%async_computation | async-start | bytes 8912896 | tf_op jit(solution)/shard_map/all_to_all | solution.py:189
  24.6 71.0 %collective-permute-done.5 = f32[2,2,32]{2,1,0:T(2,128)S(1)} collective-permute-done((f32[2,2,32]{2,1,0:T(2,128)S(1)}, f32[2,2,32]{2,1,0:T(2,128)S(1)}, u32[]{:S(2)}, u32[]{:S(2)}) %collective-permute-start.5) | collective-permute-done | bytes 544 | tf_op jit(solution)/shard_map/ppermute | solution.py:32
  95.7 5.1 %collective-permute-done.6 = f32[2,2,32]{2,1,0:T(2,128)S(1)} collective-permute-done((f32[2,2,32]{2,1,0:T(2,128)S(1)}, f32[2,2,32]{2,1,0:T(2,128)S(1)}, u32[]{:S(2)}, u32[]{:S(2)}) %collective-permute-start.6) | collective-permute-done | bytes 544 | tf_op jit(solution)/shard_map/ppermute | solution.py:32
  101.5 2.9 collective-permute-done.7
  104.3 4.7 %copy.55 = bf16[2,16,272,256]{3,2,1,0:T(8,128)(2,1)} copy(bf16[2,16,272,256]{3,2,0,1:T(8,128)(2,1)} %bitcast.20) | data formatting | bytes 8912896 | tf_op jit(solution)/shard_map/reshape | solution.py:188
  109.1 3.8 fusion.106
  114.3 2.2 copy-done.3
  117.2 25.7 %all-gather.6.cloned.1.call-done = bf16[2,4352,256]{2,0,1:T(2,128)(2,1)} async-done(((bf16[2,272,256]{2,0,1:T(2,128)(2,1)}), bf16[2,4352,256]{2,0,1:T(2,128)(2,1)}) %all-gather.6.cloned.1.call-update) | async-done | bytes 4456464 | tf_op jit(solution)/shard_map/all_gather | solution.py:178
  142.9 10.0 %fusion.19 = bf16[2,272,256]{2,1,0:T(8,128)(2,1)S(1)} fusion(bf16[2,4352,256]{2,1,0:T(8,128)(2,1)} %all-gather.4.cloned.1.call-done, f32[2,272,4352]{2,1,0:T(8,128)} %copy-done.3, bf16[2,272,256]{2,1,0:T(8,128)(2,1)S(1)} %bitcast.220, f32[2,272]{1,0:T(2,128)S(1)} %copy.65, f32[2,272]{1,0:T(2,128)S(1)} %log_add_fusion, ...), kind=kOutput, calls=%fused_computation.44 | convolution fusion | flops 2434056192 | bytes 18944256 | tf_op jit(solution)/shard_map/shqk,skhd->sqhd/dot_general | solution.py:183
  154.2 2.6 collective-permute-done.1
  156.8 2.2 collective-permute-start.2
  159.0 3.9 collective-permute-done.2
  163.6 4.6 %collective-permute-done.3 = f32[8,2,2,272,1]{3,0,2,4,1:T(8,128)S(1)} collective-permute-done((f32[8,2,2,272,1]{3,0,2,4,1:T(8,128)S(1)}, f32[8,2,2,272,1]{3,0,2,4,1:T(8,128)S(1)}, u32[]{:S(2)}, u32[]{:S(2)}) %collective-permute-start.3) | collective-permute-done | bytes 34848 | tf_op jit(solution)/shard_map/ppermute | solution.py:43
  168.5 17.4 %all-gather.8.cloned.1.call-done = bf16[2,4352,256]{2,1,0:T(8,128)(2,1)} async-done(((bf16[2,272,256]{2,1,0:T(8,128)(2,1)}), bf16[2,4352,256]{2,1,0:T(8,128)(2,1)}) %all-gather.8.cloned.1.call-update) | async-done | bytes 4456464 | tf_op jit(solution)/shard_map/all_gather | solution.py:187
  185.9 3.8 subtract_exponential_fusion
  189.7 3.7 copy-done.2
  193.4 3.7 fusion.14
  197.1 9.0 %fusion.13 = bf16[2,272,256]{2,1,0:T(8,128)(2,1)S(1)} fusion(bf16[2,4352,256]{2,1,0:T(8,128)(2,1)} %all-gather.8.cloned.1.call-done, f32[2,4352,272]{1,2,0:T(8,128)} %copy-done.2, bf16[2,4352,256]{2,1,0:T(8,128)(2,1)} %bitcast.209, f32[2,4352]{1,0:T(2,128)S(1)} %sub.121, bf16[2,272,256]{2,0,1:T(2,128)(2,1)S(1)} %bitcast.224), kind=kOutput, calls=%fused_computation.39 | convolution fusion | flops 2431688704 | bytes 18974720 | tf_op jit(solution)/shard_map/shqk,sqhd->skhd/dot_general | solution.py:197
  206.7 2.1 collective-permute-start.8
  208.8 3.6 collective-permute-start.9
  216.9 1.7 reshape.738
  218.7 1.7 reshape.737
  230.1 1.8 multiply_reduce_fusion
  232.0 6.2 %collective-permute-start.14 = (bf16[2,1,68,256]{3,2,1,0:T(8,128)(2,1)S(1)}, bf16[2,1,68,256]{3,2,1,0:T(8,128)(2,1)S(1)}, u32[]{:S(2)}, u32[]{:S(2)}) collective-permute-start(bf16[2,1,68,256]{3,2,1,0:T(8,128)(2,1)S(1)} %get-tuple-element.41), channel_id=1, source_target_pairs={{0,1},{1,2},{2,3},{3,4},{4,5},{5,6},{6,7},{7,8},{8,9},{9,10},{10,1... | collective-permute-start | bytes 208904 | tf_op jit(solution)/shard_map/ppermute | solution.py:19
  238.2 1.9 collective-permute-start.15
  249.3 2.1 convolution_add_fusion.7
  257.0 3.0 fusion.22
  261.2 2.0 fusion.30
  270.3 3.0 copy.68
  276.7 3.9 collective-permute-start.16
  280.6 3.7 collective-permute-done.16
  284.3 2.2 select_add_fusion
  287.9 13.0 %collective-permute-done.17 = f32[221184]{0:T(1024)S(1)} collective-permute-done((f32[221184]{0:T(1024)S(1)}, f32[221184]{0:T(1024)S(1)}, u32[]{:S(2)}, u32[]{:S(2)}) %collective-permute-start.17) | collective-permute-done | bytes 884768 | tf_op jit(solution)/shard_map/ppermute | solution.py:71
  300.9 1.6 select_add_fusion.1
  302.6 8.3 %collective-permute-done.18 = f32[110592]{0:T(1024)S(1)} collective-permute-done((f32[110592]{0:T(1024)S(1)}, f32[110592]{0:T(1024)S(1)}, u32[]{:S(2)}, u32[]{:S(2)}) %collective-permute-start.18) | collective-permute-done | bytes 442400 | tf_op jit(solution)/shard_map/ppermute | solution.py:71
  311.8 5.5 %collective-permute-done.19 = f32[55296]{0:T(1024)S(1)} collective-permute-done((f32[55296]{0:T(1024)S(1)}, f32[55296]{0:T(1024)S(1)}, u32[]{:S(2)}, u32[]{:S(2)}) %collective-permute-start.19) | collective-permute-done | bytes 221216 | tf_op jit(solution)/shard_map/ppermute | solution.py:71
  317.4 6.2 %collective-permute-done.20 = f32[27648]{0:T(1024)S(1)} collective-permute-done((f32[27648]{0:T(1024)S(1)}, f32[27648]{0:T(1024)S(1)}, u32[]{:S(2)}, u32[]{:S(2)}) %collective-permute-start.20) | collective-permute-done | bytes 110624 | tf_op jit(solution)/shard_map/ppermute | solution.py:71
  323.7 2.7 collective-permute-start.21
  326.5 3.0 collective-permute-done.21
  330.3 4.4 collective-permute-done.22
  334.7 2.8 collective-permute-start.23
  337.5 4.9 %collective-permute-done.23 = f32[3456]{0:T(1024)S(1)} collective-permute-done((f32[3456]{0:T(1024)S(1)}, f32[3456]{0:T(1024)S(1)}, u32[]{:S(2)}, u32[]{:S(2)}) %collective-permute-start.23) | collective-permute-done | bytes 13856 | tf_op jit(solution)/shard_map/ppermute | solution.py:71
  342.4 2.7 collective-permute-start.24
  345.2 4.9 %collective-permute-done.24 = f32[3456]{0:T(1024)S(1)} collective-permute-done((f32[3456]{0:T(1024)S(1)}, f32[3456]{0:T(1024)S(1)}, u32[]{:S(2)}, u32[]{:S(2)}) %collective-permute-start.24) | collective-permute-done | bytes 13856 | tf_op jit(solution)/shard_map/ppermute | solution.py:74
  350.6 6.0 %collective-permute-done.25 = f32[6912]{0:T(1024)S(1)} collective-permute-done((f32[6912]{0:T(1024)S(1)}, f32[6912]{0:T(1024)S(1)}, u32[]{:S(2)}, u32[]{:S(2)}) %collective-permute-start.25) | collective-permute-done | bytes 27680 | tf_op jit(solution)/shard_map/ppermute | solution.py:74
  356.6 2.8 collective-permute-start.26
  359.4 3.6 collective-permute-done.26
  363.1 7.4 %collective-permute-done.27 = f32[27648]{0:T(1024)S(1)} collective-permute-done((f32[27648]{0:T(1024)S(1)}, f32[27648]{0:T(1024)S(1)}, u32[]{:S(2)}, u32[]{:S(2)}) %collective-permute-start.27) | collective-permute-done | bytes 110624 | tf_op jit(solution)/shard_map/ppermute | solution.py:74
  370.6 8.3 %collective-permute-done.28 = f32[55296]{0:T(1024)S(1)} collective-permute-done((f32[55296]{0:T(1024)S(1)}, f32[55296]{0:T(1024)S(1)}, u32[]{:S(2)}, u32[]{:S(2)}) %collective-permute-start.28) | collective-permute-done | bytes 221216 | tf_op jit(solution)/shard_map/ppermute | solution.py:74
  379.6 7.8 %collective-permute-done.29 = f32[110592]{0:T(1024)S(1)} collective-permute-done((f32[110592]{0:T(1024)S(1)}, f32[110592]{0:T(1024)S(1)}, u32[]{:S(2)}, u32[]{:S(2)}) %collective-permute-start.29) | collective-permute-done | bytes 442400 | tf_op jit(solution)/shard_map/ppermute | solution.py:74
  388.1 13.0 %collective-permute-done.30 = f32[221184]{0:T(1024)S(1)} collective-permute-done((f32[221184]{0:T(1024)S(1)}, f32[221184]{0:T(1024)S(1)}, u32[]{:S(2)}, u32[]{:S(2)}) %collective-permute-start.30) | collective-permute-done | bytes 884768 | tf_op jit(solution)/shard_map/ppermute | solution.py:74
  403.5 2.9 collective-permute-done.10
  406.5 3.6 collective-permute-done.11
  410.1 5.1 %collective-permute-done.12 = f32[2,2,32]{2,1,0:T(2,128)S(1)} collective-permute-done((f32[2,2,32]{2,1,0:T(2,128)S(1)}, f32[2,2,32]{2,1,0:T(2,128)S(1)}, u32[]{:S(2)}, u32[]{:S(2)}) %collective-permute-start.12) | collective-permute-done | bytes 544 | tf_op jit(solution)/shard_map/ppermute | solution.py:32
  415.4 3.6 collective-permute-done.13
  423.3 1.9 concatenate.347
  425.2 2.5 maximum_select_fusion.4
  428.9 3.5 maximum_select_fusion.2
  432.3 3.0 maximum_select_fusion
  436.2 1.8 reshape.755
  439.0 1.8 concatenate.345
  440.8 1.7 fusion.37
  (267 shorter events, 68.3 us)
Async XLA Ops:
  7.2 199.0 %copy-start = (bf16[256,768]{1,0:T(8,128)(2,1)S(1)}, bf16[256,768]{1,0:T(8,128)(2,1)}, u32[]{:S(2)}) copy-start(bf16[256,768]{1,0:T(8,128)(2,1)} %param.18) | copy-start | bytes 1179652
  7.2 4.1 copy-start.30
  7.2 5.1 %copy-start.31 = (bf16[2,4,68,256]{3,1,2,0:T(4,128)(2,1)S(1)}, bf16[2,4,68,256]{3,1,2,0:T(4,128)(2,1)}, u32[]{:S(2)}) copy-start(bf16[2,4,68,256]{3,1,2,0:T(4,128)(2,1)} %param.16) | copy-start | bytes 835588
  7.2 5.2 %copy-start.35 = (bf16[256,256]{1,0:T(8,128)(2,1)S(1)}, bf16[256,256]{1,0:T(8,128)(2,1)}, u32[]{:S(2)}) copy-start(bf16[256,256]{1,0:T(8,128)(2,1)} %param.19) | copy-start | bytes 393220
  7.2 101.8 %all-gather.4.cloned.1.call-start = ((), (), s32[]{:S(2)}) async-start(), calls=%async_computation.1 | async-start | bytes 4734976 | tf_op jit(solution)/shard_map/all_gather | solution.py:177
  9.3 133.6 %all-gather.6.cloned.1.call-start = ((), (), s32[]{:S(2)}) async-start(), calls=%async_computation.2 | async-start | bytes 4734976 | tf_op jit(solution)/shard_map/all_gather | solution.py:178
  11.2 174.7 %all-gather.8.cloned.1.call-start = ((), (), s32[]{:S(2)}) async-start(), calls=%async_computation.3 | async-start | bytes 4734976 | tf_op jit(solution)/shard_map/all_gather | solution.py:187
  15.2 5.8 %copy-start.8 = (bf16[2,4,68,256]{3,1,2,0:T(4,128)(2,1)S(1)}, bf16[2,4,68,256]{3,1,2,0:T(4,128)(2,1)}, u32[]{:S(2)}) copy-start(bf16[2,4,68,256]{3,1,2,0:T(4,128)(2,1)} %param.11) | copy-start | bytes 835588
  15.2 6.5 %copy-start.32 = (bf16[2,4,68,256]{3,1,2,0:T(4,128)(2,1)S(1)}, bf16[2,4,68,256]{3,1,2,0:T(4,128)(2,1)}, u32[]{:S(2)}) copy-start(bf16[2,4,68,256]{3,1,2,0:T(4,128)(2,1)} %param.15) | copy-start | bytes 835588
  15.2 89.1 %all-to-all-start = ((bf16[16,2,272,256]{3,2,1,0:T(8,128)(2,1)}), bf16[16,2,272,256]{3,2,1,0:T(8,128)(2,1)}, u32[]{:S(2)}, u32[]{:S(2)}) async-start(bf16[16,2,272,256]{3,2,1,0:T(8,128)(2,1)} %stack.59), calls=%async_computation | async-start | bytes 8912896 | tf_op jit(solution)/shard_map/all_to_all | solution.py:189
  21.5 2.2 collective-permute-start.4
  22.4 86.7 %copy-start.11 = (f32[32,2,8,128]{3,1,2,0:T(2,128)}, f32[32,2,8,128]{3,1,2,0:T(2,128)S(1)}, u32[]{:S(2)}) copy-start(f32[32,2,8,128]{3,1,2,0:T(2,128)S(1)} %copy.67) | copy-start | bytes 786436
  23.7 71.9 %collective-permute-start.5 = (f32[2,2,32]{2,1,0:T(2,128)S(1)}, f32[2,2,32]{2,1,0:T(2,128)S(1)}, u32[]{:S(2)}, u32[]{:S(2)}) collective-permute-start(f32[2,2,32]{2,1,0:T(2,128)S(1)} %fusion.94), channel_id=1, source_target_pairs={{0,2},{1,3},{2,0},{3,1},{4,6},{5,7},{6,4},{7,5},{8,10},{9,11},{10,... | collective-permute-start | bytes 1544 | tf_op jit(solution)/shard_map/ppermute | solution.py:32
  95.7 5.1 %collective-permute-start.6 = (f32[2,2,32]{2,1,0:T(2,128)S(1)}, f32[2,2,32]{2,1,0:T(2,128)S(1)}, u32[]{:S(2)}, u32[]{:S(2)}) collective-permute-start(f32[2,2,32]{2,1,0:T(2,128)S(1)} %fusion.154), channel_id=1, source_target_pairs={{0,4},{1,5},{2,6},{3,7},{4,0},{5,1},{6,2},{7,3},{8,12},{9,13},{10,... | collective-permute-start | bytes 1544 | tf_op jit(solution)/shard_map/ppermute | solution.py:32
  100.7 3.6 collective-permute-start.7
  112.9 3.7 copy-start.3
  116.6 36.3 %collective-permute-start = (f32[1,2,2,272,1]{3,4,2,1,0:T(1,128)S(1)}, f32[1,2,2,272,1]{3,4,2,1,0:T(1,128)S(1)}, u32[]{:S(2)}, u32[]{:S(2)}) collective-permute-start(f32[1,2,2,272,1]{3,4,2,1,0:T(1,128)S(1)} %get-tuple-element.50), channel_id=1, source_target_pairs={{0,1},{1,0},{2,3},{3,2},{4,5},{5,4},{6,7},{7,6},{8,9},{9,8},{10,11... | collective-permute-start | bytes 13064 | tf_op jit(solution)/shard_map/ppermute | solution.py:43
  152.9 53.2 %copy-start.40 = (bf16[2,272,256]{2,1,0:T(8,128)(2,1)}, bf16[2,272,256]{2,1,0:T(8,128)(2,1)S(1)}, u32[]{:S(2)}) copy-start(bf16[2,272,256]{2,1,0:T(8,128)(2,1)S(1)} %fusion.19) | copy-start | bytes 835588
  153.0 3.8 collective-permute-start.1
  156.8 6.1 %collective-permute-start.2 = (f32[4,2,2,272,1]{3,0,2,1,4:T(4,128)S(1)}, f32[4,2,2,272,1]{3,0,2,1,4:T(4,128)S(1)}, u32[]{:S(2)}, u32[]{:S(2)}) collective-permute-start(f32[4,2,2,272,1]{3,0,2,1,4:T(4,128)S(1)} %maximum_select_fusion.14), channel_id=1, source_target_pairs={{0,4},{1,5},{2,6},{3,7},{4,0},{5,1},{6,2},{7,3},{8,12},{9,13},{10,... | collective-permute-start | bytes 52232 | tf_op jit(solution)/shard_map/ppermute | solution.py:43
  162.9 5.3 %collective-permute-start.3 = (f32[8,2,2,272,1]{3,0,2,4,1:T(8,128)S(1)}, f32[8,2,2,272,1]{3,0,2,4,1:T(8,128)S(1)}, u32[]{:S(2)}, u32[]{:S(2)}) collective-permute-start(f32[8,2,2,272,1]{3,0,2,4,1:T(8,128)S(1)} %fusion.81), channel_id=1, source_target_pairs={{0,8},{1,9},{2,10},{3,11},{4,12},{5,13},{6,14},{7,15},{8,0},{9,1},... | collective-permute-start | bytes 104456 | tf_op jit(solution)/shard_map/ppermute | solution.py:43
  189.7 3.7 copy-start.2
  193.4 3.7 copy-start.19
  197.1 9.0 %copy-start.28 = (bf16[2,256,272]{1,2,0:T(8,128)(2,1)}, bf16[2,256,272]{1,2,0:T(8,128)(2,1)S(1)}, u32[]{:S(2)}) copy-start(bf16[2,256,272]{1,2,0:T(8,128)(2,1)S(1)} %fusion.14) | copy-start | bytes 835588
  206.1 2.7 copy-start.33
  206.7 6.1 %collective-permute-start.8 = (bf16[2,1,68,256]{3,2,1,0:T(8,128)(2,1)S(1)}, bf16[2,1,68,256]{3,2,1,0:T(8,128)(2,1)S(1)}, u32[]{:S(2)}, u32[]{:S(2)}) collective-permute-start(bf16[2,1,68,256]{3,2,1,0:T(8,128)(2,1)S(1)} %get-tuple-element.45), channel_id=1, source_target_pairs={{0,1},{1,2},{2,3},{3,4},{4,5},{5,6},{6,7},{7,8},{8,9},{9,10},{10,1... | collective-permute-start | bytes 208904 | tf_op jit(solution)/shard_map/ppermute | solution.py:19
  208.8 5.4 %collective-permute-start.9 = (bf16[2,1,68,256]{3,2,1,0:T(8,128)(2,1)S(1)}, bf16[2,1,68,256]{3,2,1,0:T(8,128)(2,1)S(1)}, u32[]{:S(2)}, u32[]{:S(2)}) collective-permute-start(bf16[2,1,68,256]{3,2,1,0:T(8,128)(2,1)S(1)} %get-tuple-element.46), channel_id=1, source_target_pairs={{1,0},{2,1},{3,2},{4,3},{5,4},{6,5},{7,6},{8,7},{9,8},{10,9},{11,1... | collective-permute-start | bytes 208904 | tf_op jit(solution)/shard_map/ppermute | solution.py:21
  215.9 6.1 %copy-start.10 = (bf16[9,256,256]{2,1,0:T(8,128)(2,1)S(1)}, bf16[9,256,256]{2,1,0:T(8,128)(2,1)}, u32[]{:S(2)}) copy-start(bf16[9,256,256]{2,1,0:T(8,128)(2,1)} %param.17) | copy-start | bytes 3538948
  221.2 3.5 copy-start.25
  232.0 9.1 %collective-permute-start.14 = (bf16[2,1,68,256]{3,2,1,0:T(8,128)(2,1)S(1)}, bf16[2,1,68,256]{3,2,1,0:T(8,128)(2,1)S(1)}, u32[]{:S(2)}, u32[]{:S(2)}) collective-permute-start(bf16[2,1,68,256]{3,2,1,0:T(8,128)(2,1)S(1)} %get-tuple-element.41), channel_id=1, source_target_pairs={{0,1},{1,2},{2,3},{3,4},{4,5},{5,6},{6,7},{7,8},{8,9},{9,10},{10,1... | collective-permute-start | bytes 208904 | tf_op jit(solution)/shard_map/ppermute | solution.py:19
  238.2 3.9 collective-permute-start.15
  246.0 9.1 %copy-start.15 = (bf16[544,256]{1,0:T(8,128)(2,1)}, bf16[544,256]{1,0:T(8,128)(2,1)S(1)}, u32[]{:S(2)}) copy-start(bf16[544,256]{1,0:T(8,128)(2,1)S(1)} %reshape.747) | copy-start | bytes 835588
  247.2 6.6 %copy-start.17 = (bf16[544,256]{1,0:T(8,128)(2,1)}, bf16[544,256]{1,0:T(8,128)(2,1)S(1)}, u32[]{:S(2)}) copy-start(bf16[544,256]{1,0:T(8,128)(2,1)S(1)} %reshape.746) | copy-start | bytes 835588
  252.4 3.0 copy-start.13
  260.0 3.3 copy-start.18
  260.0 4.3 copy-start.16
  261.2 7.1 %copy-start.22 = (bf16[544,256]{1,0:T(8,128)(2,1)S(1)}, bf16[544,256]{1,0:T(8,128)(2,1)}, u32[]{:S(2)}) copy-start(bf16[544,256]{1,0:T(8,128)(2,1)} %reshape.751) | copy-start | bytes 835588
  263.3 6.1 %copy-start.14 = (bf16[544,256]{1,0:T(8,128)(2,1)S(1)}, bf16[544,256]{1,0:T(8,128)(2,1)}, u32[]{:S(2)}) copy-start(bf16[544,256]{1,0:T(8,128)(2,1)} %copy-done.13) | copy-start | bytes 835588
  270.3 3.0 copy-start.5
  276.7 7.6 %collective-permute-start.16 = (f32[442368]{0:T(1024)}, f32[442368]{0:T(1024)}, u32[]{:S(2)}, u32[]{:S(2)}) collective-permute-start(f32[442368]{0:T(1024)} %fusion.6), channel_id=1, source_target_pairs={{0,1},{1,0},{2,3},{3,2},{4,5},{5,4},{6,7},{7,6},{8,9},{9,8},{10,11... | collective-permute-start | bytes 5308424 | tf_op jit(solution)/shard_map/ppermute | solution.py:71
  287.8 13.1 %collective-permute-start.17 = (f32[221184]{0:T(1024)S(1)}, f32[221184]{0:T(1024)S(1)}, u32[]{:S(2)}, u32[]{:S(2)}) collective-permute-start(f32[221184]{0:T(1024)S(1)} %slice_select_fusion), channel_id=1, source_target_pairs={{0,2},{1,17},{2,0},{3,19},{4,6},{5,21},{6,4},{7,23},{8,10},{9,25},... | collective-permute-start | bytes 2654216 | tf_op jit(solution)/shard_map/ppermute | solution.py:71
  302.5 8.4 %collective-permute-start.18 = (f32[110592]{0:T(1024)S(1)}, f32[110592]{0:T(1024)S(1)}, u32[]{:S(2)}, u32[]{:S(2)}) collective-permute-start(f32[110592]{0:T(1024)S(1)} %slice_select_fusion.1), channel_id=1, source_target_pairs={{0,8},{1,3},{2,10},{3,1},{4,12},{5,7},{6,14},{7,5},{8,0},{9,11},{1... | collective-permute-start | bytes 1327112 | tf_op jit(solution)/shard_map/ppermute | solution.py:71
  311.0 6.2 %collective-permute-start.19 = (f32[55296]{0:T(1024)S(1)}, f32[55296]{0:T(1024)S(1)}, u32[]{:S(2)}, u32[]{:S(2)}) collective-permute-start(f32[55296]{0:T(1024)S(1)} %slice_select_fusion.2), channel_id=1, source_target_pairs={{0,16},{1,9},{2,18},{3,11},{4,20},{5,13},{6,22},{7,15},{8,24},{9,1... | collective-permute-start | bytes 663560 | tf_op jit(solution)/shard_map/ppermute | solution.py:71
  317.3 6.3 %collective-permute-start.20 = (f32[27648]{0:T(1024)S(1)}, f32[27648]{0:T(1024)S(1)}, u32[]{:S(2)}, u32[]{:S(2)}) collective-permute-start(f32[27648]{0:T(1024)S(1)} %slice_select_fusion.3), channel_id=1, source_target_pairs={{0,4},{1,33},{2,6},{3,35},{4,0},{5,37},{6,2},{7,39},{8,12},{9,41},... | collective-permute-start | bytes 331784 | tf_op jit(solution)/shard_map/ppermute | solution.py:71
  323.7 5.8 %collective-permute-start.21 = (f32[13824]{0:T(1024)S(1)}, f32[13824]{0:T(1024)S(1)}, u32[]{:S(2)}, u32[]{:S(2)}) collective-permute-start(f32[13824]{0:T(1024)S(1)} %slice_select_fusion.4), channel_id=1, source_target_pairs={{0,128},{1,5},{2,130},{3,7},{4,132},{5,1},{6,134},{7,3},{8,136},{9... | collective-permute-start | bytes 165896 | tf_op jit(solution)/shard_map/ppermute | solution.py:71
  329.5 5.2 %collective-permute-start.22 = (f32[6912]{0:T(1024)S(1)}, f32[6912]{0:T(1024)S(1)}, u32[]{:S(2)}, u32[]{:S(2)}) collective-permute-start(f32[6912]{0:T(1024)S(1)} %slice_select_fusion.5), channel_id=1, source_target_pairs={{0,32},{1,129},{2,34},{3,131},{4,36},{5,133},{6,38},{7,135},{8,40}... | collective-permute-start | bytes 82952 | tf_op jit(solution)/shard_map/ppermute | solution.py:71
  334.7 7.7 %collective-permute-start.23 = (f32[3456]{0:T(1024)S(1)}, f32[3456]{0:T(1024)S(1)}, u32[]{:S(2)}, u32[]{:S(2)}) collective-permute-start(f32[3456]{0:T(1024)S(1)} %slice_select_fusion.6), channel_id=1, source_target_pairs={{0,64},{1,65},{2,66},{3,67},{4,68},{5,69},{6,70},{7,71},{8,72},{9,... | collective-permute-start | bytes 41480 | tf_op jit(solution)/shard_map/ppermute | solution.py:71
  342.4 7.6 %collective-permute-start.24 = (f32[3456]{0:T(1024)S(1)}, f32[3456]{0:T(1024)S(1)}, u32[]{:S(2)}, u32[]{:S(2)}) collective-permute-start(f32[3456]{0:T(1024)S(1)} %select_add_fusion.7), channel_id=1, source_target_pairs={{0,64},{1,65},{2,66},{3,67},{4,68},{5,69},{6,70},{7,71},{8,72},{9,... | collective-permute-start | bytes 41480 | tf_op jit(solution)/shard_map/ppermute | solution.py:74
  350.1 6.5 %collective-permute-start.25 = (f32[6912]{0:T(1024)S(1)}, f32[6912]{0:T(1024)S(1)}, u32[]{:S(2)}, u32[]{:S(2)}) collective-permute-start(f32[6912]{0:T(1024)S(1)} %maximum_select_fusion.13), channel_id=1, source_target_pairs={{0,32},{1,129},{2,34},{3,131},{4,36},{5,133},{6,38},{7,135},{8,40}... | collective-permute-start | bytes 82952 | tf_op jit(solution)/shard_map/ppermute | solution.py:74
  356.6 6.4 %collective-permute-start.26 = (f32[13824]{0:T(1024)S(1)}, f32[13824]{0:T(1024)S(1)}, u32[]{:S(2)}, u32[]{:S(2)}) collective-permute-start(f32[13824]{0:T(1024)S(1)} %maximum_select_fusion.10), channel_id=1, source_target_pairs={{0,128},{1,5},{2,130},{3,7},{4,132},{5,1},{6,134},{7,3},{8,136},{9... | collective-permute-start | bytes 165896 | tf_op jit(solution)/shard_map/ppermute | solution.py:74
  363.0 7.5 %collective-permute-start.27 = (f32[27648]{0:T(1024)S(1)}, f32[27648]{0:T(1024)S(1)}, u32[]{:S(2)}, u32[]{:S(2)}) collective-permute-start(f32[27648]{0:T(1024)S(1)} %maximum_select_fusion.8), channel_id=1, source_target_pairs={{0,4},{1,33},{2,6},{3,35},{4,0},{5,37},{6,2},{7,39},{8,12},{9,41},... | collective-permute-start | bytes 331784 | tf_op jit(solution)/shard_map/ppermute | solution.py:74
  370.5 8.4 %collective-permute-start.28 = (f32[55296]{0:T(1024)S(1)}, f32[55296]{0:T(1024)S(1)}, u32[]{:S(2)}, u32[]{:S(2)}) collective-permute-start(f32[55296]{0:T(1024)S(1)} %maximum_select_fusion.7), channel_id=1, source_target_pairs={{0,16},{1,9},{2,18},{3,11},{4,20},{5,13},{6,22},{7,15},{8,24},{9,1... | collective-permute-start | bytes 663560 | tf_op jit(solution)/shard_map/ppermute | solution.py:74
  378.9 23.8 %copy-start.36 = (f32[2,256]{1,0:T(2,128)S(1)}, f32[2,256]{1,0:T(2,128)}, u32[]{:S(2)}) copy-start(f32[2,256]{1,0:T(2,128)} %get-tuple-element.20) | copy-start | bytes 6148
  379.0 8.4 %collective-permute-start.29 = (f32[110592]{0:T(1024)S(1)}, f32[110592]{0:T(1024)S(1)}, u32[]{:S(2)}, u32[]{:S(2)}) collective-permute-start(f32[110592]{0:T(1024)S(1)} %maximum_select_fusion.5), channel_id=1, source_target_pairs={{0,8},{1,3},{2,10},{3,1},{4,12},{5,7},{6,14},{7,5},{8,0},{9,11},{1... | collective-permute-start | bytes 1327112 | tf_op jit(solution)/shard_map/ppermute | solution.py:74
  388.1 31.2 %copy-start.9 = (bf16[2,4,68,256]{3,1,2,0:T(4,128)(2,1)S(1)}, bf16[2,4,68,256]{3,1,2,0:T(4,128)(2,1)}, u32[]{:S(2)}) copy-start(bf16[2,4,68,256]{3,1,2,0:T(4,128)(2,1)} %param.11) | copy-start | bytes 835588
  388.1 31.2 %copy-start.38 = (f32[256]{0:T(256)S(1)}, f32[256]{0:T(256)}, u32[]{:S(2)}) copy-start(f32[256]{0:T(256)} %param.20) | copy-start | bytes 3076
  388.1 13.0 %collective-permute-start.30 = (f32[221184]{0:T(1024)S(1)}, f32[221184]{0:T(1024)S(1)}, u32[]{:S(2)}, u32[]{:S(2)}) collective-permute-start(f32[221184]{0:T(1024)S(1)} %maximum_select_fusion.3), channel_id=1, source_target_pairs={{0,2},{1,17},{2,0},{3,19},{4,6},{5,21},{6,4},{7,23},{8,10},{9,25},... | collective-permute-start | bytes 2654216 | tf_op jit(solution)/shard_map/ppermute | solution.py:74
  402.6 29.8 %collective-permute-start.31 = (f32[442368]{0:T(1024)}, f32[442368]{0:T(1024)S(1)}, u32[]{:S(2)}, u32[]{:S(2)}) collective-permute-start(f32[442368]{0:T(1024)} %maximum_select_fusion.1), channel_id=1, source_target_pairs={{0,1},{1,0},{2,3},{3,2},{4,5},{5,4},{6,7},{7,6},{8,9},{9,8},{10,11... | collective-permute-start | bytes 5308424 | tf_op jit(solution)/shard_map/ppermute | solution.py:74
  403.0 3.5 collective-permute-start.10
  406.5 3.6 collective-permute-start.11
  410.1 5.1 %collective-permute-start.12 = (f32[2,2,32]{2,1,0:T(2,128)S(1)}, f32[2,2,32]{2,1,0:T(2,128)S(1)}, u32[]{:S(2)}, u32[]{:S(2)}) collective-permute-start(f32[2,2,32]{2,1,0:T(2,128)S(1)} %fusion.153), channel_id=1, source_target_pairs={{0,4},{1,5},{2,6},{3,7},{4,0},{5,1},{6,2},{7,3},{8,12},{9,13},{10,... | collective-permute-start | bytes 1544 | tf_op jit(solution)/shard_map/ppermute | solution.py:32
  415.2 3.8 collective-permute-start.13
  432.3 3.0 copy-start.7
  438.9 3.5 copy-start.1
  (13 other events, 22.4 us)
Sparse Core Ops, SparseCore 0:
  10.4 88.3 all-gather.3
  101.2 41.6 all-gather.5
  145.3 40.6 all-gather.7
